TPU v7x, 128 devices: a whole 4x4x4 slice. The times are simulated.
128 devices in a mesh: dp: 8 (over z, core), seq: 16 (over y, x).
Axes of the slice: x: 4, y: 4, z: 4, core: 2. Of those that a mesh axis runs over, the one named last changes fastest.
Arguments:
- tokens: bfloat16 [8, 8192, 2048], P('dp', 'seq'), may hold values from -6 to 6
- input_gain: bfloat16 [2048], replicated, may hold values from 0.099609375 to 1.8984375
- qkv_weight: bfloat16 [2048, 6144], P(None, ('dp', 'seq')), may hold values from -0.125 to 0.125
- head_gain: bfloat16 [2048], replicated, may hold values from 0.099609375 to 1.8984375
- prefix_state: float32 [8, 16, 128, 128], P('dp'), may hold values from -256 to 256
Outputs:
- attended: bfloat16 [8, 8192, 2048], P('dp', 'seq')
All inputs are finite; a program needn't handle non-finite values.
Results may differ from a plain program's by a relative error of at most 0.0061.
Values may be sent and summed in bfloat16 or wider, within the bound.
No kernel may reach another device: no remote copies, remote signals or barrier semaphores. Data moves between devices by JAX's collectives and lax.ppermute only.
A program may use at most 128 MiB of HBM per device.

v0:
```python
import jax
import jax.numpy as jnp
from jax import lax
from jax.sharding import PartitionSpec as P

D = 2048
H = 16
DH = 128
BLOCK = 512
epsilon = 1e-05


def feature_map(inputs):
    return jnp.where(inputs > 0, inputs + 1.0, jnp.exp(jnp.minimum(inputs, 0.0)))


def span_attention(queries, key_feats, values, memory, head_gain):
    num_blocks = queries.shape[0] // BLOCK
    causal = jnp.arange(BLOCK)[:, None] >= jnp.arange(BLOCK)[None, :]
    gains = head_gain.astype(jnp.float32).reshape(H, DH)

    def advance(running, blocks):
        query_blk, key_blk, value_blk = blocks
        carried = jnp.einsum(
            "bhd,hde->bhe",
            query_blk,
            running.astype(jnp.bfloat16),
            preferred_element_type=jnp.float32,
        )
        scores = jnp.einsum("bhd,chd->hbc", query_blk, key_blk, preferred_element_type=jnp.float32)
        scores = jnp.where(causal[None], scores, 0.0).astype(jnp.bfloat16)
        within = jnp.einsum("hbc,che->bhe", scores, value_blk, preferred_element_type=jnp.float32)
        numerator = carried + within
        scale = lax.rsqrt(jnp.mean(numerator * numerator, axis=-1, keepdims=True) + epsilon)
        running = running + jnp.einsum(
            "bhd,bhe->hde", key_blk, value_blk, preferred_element_type=jnp.float32
        )
        return (running, (numerator * scale * gains).astype(jnp.bfloat16))

    def shaped(inputs):
        return inputs.reshape(num_blocks, BLOCK, H, DH)

    final_memory, outputs = lax.scan(
        advance, memory, (shaped(queries), shaped(key_feats), shaped(values))
    )
    return outputs.reshape(num_blocks * BLOCK, H * DH)


def body(tokens, input_gain, qkv_weight, head_gain, prefix_state):
    inputs = tokens[0].astype(jnp.float32)
    normed = inputs * lax.rsqrt(jnp.mean(inputs * inputs, axis=-1, keepdims=True) + epsilon)
    normed = (normed * input_gain.astype(jnp.float32)).astype(jnp.bfloat16)
    tok_rows = normed.shape[0]
    projected = jnp.dot(
        normed,
        lax.all_gather(qkv_weight, ("dp", "seq"), axis=1, tiled=True),
        preferred_element_type=jnp.float32,
    )
    queries = feature_map(projected[:, :D]).astype(jnp.bfloat16).reshape(tok_rows, H, DH)
    key_feats = feature_map(projected[:, D : 2 * D]).astype(jnp.bfloat16).reshape(tok_rows, H, DH)
    values = projected[:, 2 * D :].astype(jnp.bfloat16).reshape(tok_rows, H, DH)
    local = jnp.einsum(
        "thd,the->hde", key_feats, values, preferred_element_type=jnp.float32
    ).astype(jnp.bfloat16)
    gathered = lax.all_gather(local[None], "seq", axis=0, tiled=True)
    my_index = lax.axis_index("seq")
    earlier = (jnp.arange(gathered.shape[0]) < my_index).astype(jnp.bfloat16)
    before = jnp.einsum("c,chde->hde", earlier, gathered, preferred_element_type=jnp.float32)
    memory = prefix_state[0] + before
    attended = span_attention(queries, key_feats, values, memory, head_gain)
    return attended[None]


def solution(mesh):
    placed = (P("dp", "seq", None), P(), P(None, ("dp", "seq")), P(), P("dp", None, None, None))
    return jax.shard_map(
        body, mesh=mesh, in_specs=placed, out_specs=P("dp", "seq", None), check_vma=False
    )
```

profile of v0, /device:TPU:1, one launch (start us, length us, event | category | flops | bytes accessed | tf_op | source)
XLA Modules:
  0.0 235.7 jit_solution(6228382882600847953)
XLA Ops:
  6.5 0.0 all-gather.4.cloned.1.call-start
  6.5 0.7 all-gather.4.cloned.1.call-update
  7.3 0.0 all-gather.6.cloned.1.call-start
  7.3 0.7 convert_element_type.38
  8.0 2.1 fusion.2
  10.1 97.0 %all-gather.4.cloned.1.call-done = bf16[2048,6144]{0,1:T(8,128)(2,1)} async-done(((bf16[2048,48]{0,1:T(8,128)(2,1)}), bf16[2048,6144]{0,1:T(8,128)(2,1)}) %all-gather.4.cloned.1.call-update) | async-done | bytes 25165840 | tf_op jit(solution)/shard_map/all_gather | solution.py:56
  107.1 20.0 %fusion.10 = f32[512,6144]{1,0:T(8,128)} fusion(bf16[2048,6144]{0,1:T(8,128)(2,1)} %all-gather.4.cloned.1.call-done, bf16[1,512,2048]{2,1,0:T(8,128)(2,1)} %param.5, f32[2048]{0:T(1024)S(1)} %convert_element_type.38, f32[512]{0:T(512)S(1)} %add_rsqrt_fusion.1), kind=kOutput, calls=%fused_computation.19 | convolution fusion | flops 12889096192 | bytes 39856128 | tf_op jit(solution)/shard_map/dot_general | solution.py:54
  127.1 5.7 %fusion.9 = (bf16[64,16,8,128]{3,2,1,0:T(8,128)(2,1)}, bf16[512,2048]{1,0:T(8,128)(2,1)}) fusion(f32[512,6144]{1,0:T(8,128)} %fusion.10), kind=kLoop, calls=%fused_computation.18 | loop fusion | flops 10485760 | bytes 12582912
  132.8 3.8 %slice.21 = bf16[512,2048]{1,0:T(8,128)(2,1)} slice(f32[512,6144]{1,0:T(8,128)} %fusion.10), slice={[0:512], [4096:6144]} | slice | bytes 4194304 | tf_op jit(solution)/shard_map/slice | solution.py:61
  136.6 2.9 %copy.22 = bf16[512,2048]{0,1:T(8,128)(2,1)S(1)} copy(bf16[512,2048]{1,0:T(8,128)(2,1)} %get-tuple-element.20) | data formatting | bytes 4194304 | tf_op jit(solution)/shard_map/reshape | solution.py:60
  139.5 0.0 copy-start.3
  139.5 4.0 %copy.23 = bf16[512,2048]{0,1:T(8,128)(2,1)} copy(bf16[512,2048]{1,0:T(8,128)(2,1)} %slice.21) | data formatting | bytes 4194304 | tf_op jit(solution)/shard_map/reshape | solution.py:61
  143.5 3.1 %convolution_convert_fusion = bf16[16,128,128]{2,1,0:T(8,128)(2,1)} fusion(bf16[512,16,128]{0,2,1:T(8,128)(2,1)S(1)} %bitcast.53, bf16[512,16,128]{0,2,1:T(8,128)(2,1)} %bitcast.55), kind=kOutput, calls=%fused_computation.27 | convolution fusion | flops 268697600 | bytes 4718592 | tf_op jit(solution)/shard_map/thd,the->hde/dot_general | solution.py:62
  146.6 0.0 all-gather.6.cloned.1.call-update
  146.6 0.1 iota_compare_fusion
  146.7 0.0 copy-done.3
  146.7 9.2 %fusion.8 = f32[16,128,512]{2,1,0:T(8,128)} fusion(bf16[512,16,128]{0,2,1:T(8,128)(2,1)} %bitcast.56, bf16[512,16,128]{0,2,1:T(8,128)(2,1)S(1)} %bitcast.54, pred[512,512]{1,0:T(8,128)(4,1)S(1)} %iota_compare_fusion, bf16[64,16,8,128]{3,2,1,0:T(8,128)(2,1)} %get-tuple-element.19), kind=kOutput, calls=%fused_computation.16 | convolution fusion | flops 2155872256 | bytes 10747904 | tf_op jit(solution)/shard_map/while/body/eval_jaxpr/hbc,che->bhe/dot_general | solution.py:32
  155.9 60.4 %all-gather.6.cloned.1.call-done = bf16[256,128,128]{2,1,0:T(8,128)(2,1)} async-done(((bf16[16,128,128]{2,1,0:T(8,128)(2,1)}), bf16[256,128,128]{2,1,0:T(8,128)(2,1)}) %all-gather.6.cloned.1.call-update) | async-done | bytes 8388624 | tf_op jit(solution)/shard_map/all_gather | solution.py:65
  216.3 0.0 copy-start
  216.3 0.0 copy-start.1
  216.3 0.0 copy-start.2
  216.3 8.4 %fusion = f32[1,16,128,128]{3,0,2,1:T(1,128)S(1)} fusion(bf16[16,16,128,128]{3,2,1,0:T(8,128)(2,1)} %bitcast.52, s32[]{:T(128)S(6)} %axis_index.12), kind=kOutput, calls=%fused_computation.1 | convolution fusion | flops 8388624 | bytes 9437188 | tf_op jit(solution)/shard_map/c,chde->hde/dot_general | solution.py:68
  224.8 0.0 copy-done
  224.8 0.0 copy-done.1
  224.8 0.0 copy-done.2
  224.8 1.0 fusion.5
  225.9 0.6 fusion.7
  226.5 2.4 %copy.17 = bf16[1,512,2048]{2,1,0:T(8,128)(2,1)} copy(bf16[1,512,2048]{1,2,0:T(8,128)(2,1)S(1)} %bitcast.57) | data formatting | bytes 4194304 | tf_op jit(solution)/shard_map/broadcast_in_dim;reshape | solution.py:71
  (3 shorter events, 0.0 us)
Async XLA Ops:
  6.5 100.6 %all-gather.4.cloned.1.call-start = ((), (), s32[]{:S(2)}) async-start(), calls=%async_computation | async-start | bytes 25362432 | tf_op jit(solution)/shard_map/all_gather | solution.py:56
  7.3 209.1 %all-gather.6.cloned.1.call-start = ((), (), s32[]{:S(2)}) async-start(), calls=%async_computation.1 | async-start | bytes 8912896 | tf_op jit(solution)/shard_map/all_gather | solution.py:65
  139.5 7.2 %copy-start.3 = (bf16[2048]{0:T(1024)(128)(2,1)S(1)}, bf16[2048]{0:T(1024)(128)(2,1)}, u32[]{:S(2)}) copy-start(bf16[2048]{0:T(1024)(128)(2,1)} %param.8) | copy-start | bytes 12292
  216.3 8.5 %copy-start = (bf16[64,16,8,128]{3,2,1,0:T(8,128)(2,1)S(1)}, bf16[64,16,8,128]{3,2,1,0:T(8,128)(2,1)}, u32[]{:S(2)}) copy-start(bf16[64,16,8,128]{3,2,1,0:T(8,128)(2,1)} %get-tuple-element.19) | copy-start | bytes 6291460
  216.3 8.5 %copy-start.1 = (f32[16,128,512]{2,1,0:T(8,128)S(1)}, f32[16,128,512]{2,1,0:T(8,128)}, u32[]{:S(2)}) copy-start(f32[16,128,512]{2,1,0:T(8,128)} %fusion.8) | copy-start | bytes 12582916
  216.3 8.5 %copy-start.2 = (f32[1,16,128,128]{3,2,1,0:T(8,128)S(1)}, f32[1,16,128,128]{3,2,1,0:T(8,128)}, u32[]{:S(2)}) copy-start(f32[1,16,128,128]{3,2,1,0:T(8,128)} %param.9) | copy-start | bytes 3145732
Sparse Core Ops, SparseCore 0:
  10.4 96.6 all-gather.3
  146.7 69.5 all-gather.5
where the time goes:
time: 236 us
  waiting for transfers between devices  158 us (67%)
  matrix products  41.8 us (18%)
  between operations  13.5 us (6%)
  local copies, waits for them, and re-layouts  13 us (6%)
  other arithmetic  9.23 us (4%)
    all_gather x1, waiting for transfers between devices, body(): lax.all_gather(qkv_weight, ('dp', 'seq'), axis=1, tiled=True)  97 us
    all_gather x1, waiting for transfers between devices, body(): gathered = lax.all_gather(local[None], 'seq', axis=0, tiled=True)  60.4 us
    dot_general x1, matrix products, body(): jnp.dot(normed, lax.all_gather(qkv_weight, ('dp', 'seq'), axis=1, tiled=T...  20 us
    dot_general x1, matrix products, advance(): jnp.einsum('hbc,che->bhe', scores, value_blk, preferred_element_type=jnp....  9.24 us
    dot_general x1, matrix products, body(): jnp.einsum('c,chde->hde', earlier, gathered, preferred_element_type=jnp.f...  8.45 us
    unnamed x1, other arithmetic  5.73 us
  transfers between devices with their start and end apart: 2, of which 2 were waited for; matrix products, arithmetic and copies ran while one was open for 5% of the time, Pallas kernels for 0%

commit v1 on v0

--- a/solution.py
+++ b/solution.py
@@ -62,7 +62,9 @@
     local = jnp.einsum(
         "thd,the->hde", key_feats, values, preferred_element_type=jnp.float32
     ).astype(jnp.bfloat16)
-    gathered = lax.all_gather(local[None], "seq", axis=0, tiled=True)
+    gathered = jnp.concatenate(
+        lax.all_to_all(jnp.stack([local[None]] * lax.axis_size("seq")), "seq", 0, 0), axis=0
+    )
     my_index = lax.axis_index("seq")
     earlier = (jnp.arange(gathered.shape[0]) < my_index).astype(jnp.bfloat16)
     before = jnp.einsum("c,chde->hde", earlier, gathered, preferred_element_type=jnp.float32)

time: 236 us -> 303 us (1.28)
  waiting for transfers between devices: 158 us -> 213 us
  starting transfers between devices: 0.04 us -> 6.73 us
  local copies, waits for them, and re-layouts: 13 us -> 18.5 us
    all_to_all x0 -> x1, waiting for transfers between devices: none -> 116 us  [body(): lax.all_to_all(jnp.stack([local[None]] * lax.axis_size('seq')), 'seq', 0, 0)]
    all_gather x1 -> x0, waiting for transfers between devices: 60.4 us -> none  [body(): gathered = lax.all_gather(local[None], 'seq', axis=0, tiled=True)]
    all_to_all x0 -> x1, starting transfers between devices: none -> 6.73 us  [body(): lax.all_to_all(jnp.stack([local[None]] * lax.axis_size('seq')), 'seq', 0, 0)]
    another operation x0 -> x1, local copies, waits for them, and re-layouts: none -> 5.43 us  [body(): jnp.stack([local[None]] * lax.axis_size('seq'))]
  transfers between devices with their start and end apart: 2 -> 2, of which waited for: 2 -> 2; matrix products, arithmetic and copies ran while one was open for 5% -> 4% of each run, Pallas kernels for 0% -> 0%
where the time goes in v1:
time: 303 us; the launch traced here: 302 us
  waiting for transfers between devices  213 us (70%)
  matrix products  40.9 us (13%)
  local copies, waits for them, and re-layouts  18.5 us (6%)
  between operations  13.5 us (4%)
  other arithmetic  9.25 us (3%)
  starting transfers between devices  6.73 us (2%)
    all_to_all x1, waiting for transfers between devices, body(): lax.all_to_all(jnp.stack([local[None]] * lax.axis_size('seq')), 'seq', 0, 0)  116 us
    all_gather x1, waiting for transfers between devices, body(): lax.all_gather(qkv_weight, ('dp', 'seq'), axis=1, tiled=True)  97.1 us
    dot_general x1, matrix products, body(): jnp.dot(normed, lax.all_gather(qkv_weight, ('dp', 'seq'), axis=1, tiled=T...  19.9 us
    dot_general x1, matrix products, advance(): jnp.einsum('hbc,che->bhe', scores, value_blk, preferred_element_type=jnp....  9.21 us
    dot_general x1, matrix products, body(): jnp.einsum('c,chde->hde', earlier, gathered, preferred_element_type=jnp.f...  8.45 us
    all_to_all x1, starting transfers between devices, body(): lax.all_to_all(jnp.stack([local[None]] * lax.axis_size('seq')), 'seq', 0, 0)  6.73 us
  transfers between devices with their start and end apart: 2, of which 2 were waited for; matrix products, arithmetic and copies ran while one was open for 4% of the time, Pallas kernels for 0%

profile of v1, /device:TPU:1, one launch (start us, length us, event | category | flops | bytes accessed | tf_op | source)
XLA Modules:
  0.0 302.3 jit_solution(12597458500313309577)
XLA Ops:
  6.5 0.0 all-gather.2.cloned.1.call-start
  6.5 0.7 all-gather.2.cloned.1.call-update
  7.3 0.7 convert_element_type.38
  7.9 2.1 fusion.2
  10.0 97.1 %all-gather.2.cloned.1.call-done = bf16[2048,6144]{0,1:T(8,128)(2,1)} async-done(((bf16[2048,48]{0,1:T(8,128)(2,1)}), bf16[2048,6144]{0,1:T(8,128)(2,1)}) %all-gather.2.cloned.1.call-update) | async-done | bytes 25165840 | tf_op jit(solution)/shard_map/all_gather | solution.py:56
  107.1 19.9 %fusion.10 = f32[512,6144]{1,0:T(8,128)} fusion(bf16[2048,6144]{0,1:T(8,128)(2,1)} %all-gather.2.cloned.1.call-done, bf16[1,512,2048]{2,1,0:T(8,128)(2,1)} %param.5, f32[2048]{0:T(1024)S(1)} %convert_element_type.38, f32[512]{0:T(512)S(1)} %add_rsqrt_fusion.1), kind=kOutput, calls=%fused_computation.19 | convolution fusion | flops 12889096192 | bytes 39856128 | tf_op jit(solution)/shard_map/dot_general | solution.py:54
  127.0 5.7 %fusion.9 = (bf16[64,16,8,128]{3,2,1,0:T(8,128)(2,1)}, bf16[512,2048]{1,0:T(8,128)(2,1)}) fusion(f32[512,6144]{1,0:T(8,128)} %fusion.10), kind=kLoop, calls=%fused_computation.18 | loop fusion | flops 10485760 | bytes 12582912
  132.8 3.8 %slice.21 = bf16[512,2048]{1,0:T(8,128)(2,1)} slice(f32[512,6144]{1,0:T(8,128)} %fusion.10), slice={[0:512], [4096:6144]} | slice | bytes 4194304 | tf_op jit(solution)/shard_map/slice | solution.py:61
  136.6 2.9 copy.16
  139.5 4.0 %copy.17 = bf16[512,2048]{0,1:T(8,128)(2,1)} copy(bf16[512,2048]{1,0:T(8,128)(2,1)} %slice.21) | data formatting | bytes 4194304 | tf_op jit(solution)/shard_map/reshape | solution.py:61
  143.4 2.3 convolution_convert_fusion
  145.7 5.4 %stack.3 = bf16[16,1,16,128,128]{4,3,2,1,0:T(8,128)(2,1)} broadcast(bf16[16,128,128]{2,1,0:T(8,128)(2,1)S(1)} %convolution_convert_fusion), dimensions={2,3,4} | broadcast | bytes 8912896 | tf_op jit(solution)/shard_map/stack | solution.py:66
  151.2 0.0 copy-start.3
  151.2 6.7 %all-to-all-start = ((bf16[16,1,16,128,128]{4,3,2,1,0:T(8,128)(2,1)}), bf16[16,1,16,128,128]{4,3,2,1,0:T(8,128)(2,1)}, u32[]{:S(2)}, u32[]{:S(2)}) async-start(bf16[16,1,16,128,128]{4,3,2,1,0:T(8,128)(2,1)} %stack.3), calls=%async_computation | async-start | bytes 16777216 | tf_op jit(solution)/shard_map/all_to_all | solution.py:66
  157.9 0.1 iota_compare_fusion
  158.0 0.0 copy-done.3
  158.0 9.2 %fusion.8 = f32[16,128,512]{2,1,0:T(8,128)} fusion(bf16[512,16,128]{0,2,1:T(8,128)(2,1)} %bitcast.55, bf16[512,16,128]{0,2,1:T(8,128)(2,1)S(1)} %bitcast.53, pred[512,512]{1,0:T(8,128)(4,1)S(1)} %iota_compare_fusion, bf16[64,16,8,128]{3,2,1,0:T(8,128)(2,1)} %get-tuple-element.19), kind=kOutput, calls=%fused_computation.16 | convolution fusion | flops 2155872256 | bytes 10747904 | tf_op jit(solution)/shard_map/while/body/eval_jaxpr/hbc,che->bhe/dot_general | solution.py:32
  167.2 115.6 %all-to-all-done = bf16[16,1,16,128,128]{4,3,2,1,0:T(8,128)(2,1)} async-done(((bf16[16,1,16,128,128]{4,3,2,1,0:T(8,128)(2,1)}), bf16[16,1,16,128,128]{4,3,2,1,0:T(8,128)(2,1)}, u32[]{:S(2)}, u32[]{:S(2)}) %all-to-all-start) | async-done | bytes 8388640 | tf_op jit(solution)/shard_map/all_to_all | solution.py:66
  282.9 0.0 copy-start
  282.9 0.0 copy-start.1
  282.9 0.0 copy-start.2
  282.9 8.4 %fusion = f32[1,16,128,128]{3,0,2,1:T(1,128)S(1)} fusion(bf16[16,16,128,128]{3,2,1,0:T(8,128)(2,1)} %bitcast.6, s32[]{:T(128)S(6)} %axis_index.12), kind=kOutput, calls=%fused_computation.1 | convolution fusion | flops 8388624 | bytes 9437188 | tf_op jit(solution)/shard_map/c,chde->hde/dot_general | solution.py:70
  291.3 0.0 copy-done
  291.3 0.0 copy-done.1
  291.3 0.0 copy-done.2
  291.3 1.0 fusion.5
  292.4 0.6 fusion.7
  293.0 2.4 copy.11
  (3 shorter events, 0.0 us)
Async XLA Ops:
  6.5 100.6 %all-gather.2.cloned.1.call-start = ((), (), s32[]{:S(2)}) async-start(), calls=%async_computation.1 | async-start | bytes 25362432 | tf_op jit(solution)/shard_map/all_gather | solution.py:56
  151.2 6.8 %copy-start.3 = (bf16[2048]{0:T(1024)(128)(2,1)S(1)}, bf16[2048]{0:T(1024)(128)(2,1)}, u32[]{:S(2)}) copy-start(bf16[2048]{0:T(1024)(128)(2,1)} %param.8) | copy-start | bytes 12292
  151.2 131.7 %all-to-all-start = ((bf16[16,1,16,128,128]{4,3,2,1,0:T(8,128)(2,1)}), bf16[16,1,16,128,128]{4,3,2,1,0:T(8,128)(2,1)}, u32[]{:S(2)}, u32[]{:S(2)}) async-start(bf16[16,1,16,128,128]{4,3,2,1,0:T(8,128)(2,1)} %stack.3), calls=%async_computation | async-start | bytes 16777216 | tf_op jit(solution)/shard_map/all_to_all | solution.py:66
  282.9 8.5 %copy-start = (bf16[64,16,8,128]{3,2,1,0:T(8,128)(2,1)S(1)}, bf16[64,16,8,128]{3,2,1,0:T(8,128)(2,1)}, u32[]{:S(2)}) copy-start(bf16[64,16,8,128]{3,2,1,0:T(8,128)(2,1)} %get-tuple-element.19) | copy-start | bytes 6291460
  282.9 8.5 %copy-start.1 = (f32[16,128,512]{2,1,0:T(8,128)S(1)}, f32[16,128,512]{2,1,0:T(8,128)}, u32[]{:S(2)}) copy-start(f32[16,128,512]{2,1,0:T(8,128)} %fusion.8) | copy-start | bytes 12582916
  282.9 8.5 %copy-start.2 = (f32[1,16,128,128]{3,2,1,0:T(8,128)S(1)}, f32[1,16,128,128]{3,2,1,0:T(8,128)}, u32[]{:S(2)}) copy-start(f32[1,16,128,128]{3,2,1,0:T(8,128)} %param.9) | copy-start | bytes 3145732
Sparse Core Ops, SparseCore 0:
  10.4 96.6 all-gather.1
